TPU v7x, 512 devices: a whole 4x8x8 slice. The times are simulated.
512 devices in a mesh: row: 32 (over z_hi, x, core), col: 16 (over z_lo, y).
Axes of the slice: x: 4, y: 8, z: 8 (z_hi: 4, z_lo: 2; z = z_hi * 2 + z_lo), core: 2. Of those that a mesh axis runs over, the one named last changes fastest.
Arguments:
- amps: float32 [32, 4, 576, 576], P(None, None, 'row', 'col'), may hold values from -6 to 6
- integrals: float32 [4, 576, 32, 576], P(None, 'row', 'col'), may hold values from -0.5 to 0.5
- e_occ: float32 [32], replicated, may hold values from -2 to -0.5
- e_vir: float32 [576], replicated, may hold values from 0.5 to 3
Outputs:
- update: float32 [32, 32, 576, 576], P('row', 'col')
All inputs are finite; a program needn't handle non-finite values.
Results may differ from a plain program's by a relative error of at most 0.00007.
Values sent between devices are 32-bit elements; how exact they have to be, the bound alone decides.
No kernel may reach another device: no remote copies, remote signals or barrier semaphores. Data moves between devices by JAX's collectives and lax.ppermute only.
A program may use at most 128 MiB of HBM per device.

v0:
```python
import jax
import jax.numpy as jnp
from jax import lax
from jax.sharding import PartitionSpec as P


def contract(left, right):
    return jnp.einsum(
        "ikac,kcjb->ijab",
        left,
        right,
        precision=lax.Precision.HIGHEST,
        preferred_element_type=jnp.float32,
    )


def shards(amps, integrals, e_occ, e_vir):
    row_count = lax.axis_size("row")
    col_count = lax.axis_size("col")
    row_index = lax.axis_index("row")
    col_index = lax.axis_index("col")
    occ_col = e_occ.shape[0] // col_count
    vir_row = e_vir.shape[0] // row_count
    a_energy = lax.dynamic_slice_in_dim(e_vir, row_index * vir_row, vir_row)
    j_energy = lax.dynamic_slice_in_dim(e_occ, col_index * occ_col, occ_col)
    gathered = lax.all_gather(integrals, "row", axis=1, tiled=True)
    contracted = contract(lax.all_gather(amps, "col", axis=3, tiled=True), gathered)
    denom = (
        e_occ[:, None, None, None]
        + j_energy[None, :, None, None]
        - a_energy[None, None, :, None]
        - e_vir[None, None, None, :]
    )
    scaled = contracted / denom
    scaled = lax.all_to_all(scaled, "row", split_axis=0, concat_axis=2, tiled=True)
    return scaled


def solution(mesh):
    placed = (P(None, None, "row", "col"), P(None, "row", "col", None), P(), P())
    return jax.shard_map(
        shards, mesh=mesh, in_specs=placed, out_specs=P("row", "col", None, None), check_vma=False
    )
```

profile of v0, /device:TPU:1, one launch (start us, length us, event | category | flops | bytes accessed | tf_op | source)
XLA Modules:
  0.0 468.0 jit_solution(11950487437803002496)
XLA Ops:
  6.5 0.0 copy-start
  6.5 0.0 copy-start.2
  6.5 0.0 copy-start.1
  6.5 0.0 all-gather.5.cloned.1.call-start
  6.5 2.6 copy.19
  9.2 0.0 all-gather.5.cloned.1.call-update
  9.2 0.0 all-gather.3.cloned.1.call-start
  9.3 0.0 copy-done
  9.3 0.8 copy.18
  10.1 0.0 all-gather.3.cloned.1.call-update
  10.1 0.0 copy-done.2
  10.1 0.1 dynamic_slice.7
  10.2 0.0 copy-done.1
  10.2 0.1 dynamic_slice.6
  10.3 0.1 broadcast_add_fusion
  10.4 0.1 broadcast_subtract_fusion
  10.4 237.1 %all-gather.5.cloned.1.call-done = f32[32,4,18,576]{0,1,2,3:T(4,128)} async-done(((f32[32,4,18,36]{0,1,2,3:T(4,128)}), f32[32,4,18,576]{0,1,2,3:T(4,128)}) %all-gather.5.cloned.1.call-update) | async-done | bytes 5308432 | tf_op jit(solution)/shard_map/all_gather | solution.py:27
  247.5 18.0 %copy.21 = f32[32,4,18,576]{3,0,1,2:T(8,128)} copy(f32[32,4,18,576]{0,1,2,3:T(4,128)} %all-gather.5.cloned.1.call-done) | data formatting | bytes 10616832 | tf_op jit(solution)/shard_map/all_gather | solution.py:27
  265.5 84.8 %all-gather.3.cloned.1.call-done = f32[4,576,2,576]{3,0,2,1:T(4,128)} async-done(((f32[4,18,2,576]{3,0,2,1:T(4,128)}), f32[4,576,2,576]{3,0,2,1:T(4,128)}) %all-gather.3.cloned.1.call-update) | async-done | bytes 10616848 | tf_op jit(solution)/shard_map/all_gather | solution.py:26
  350.2 31.1 %bitcast_divide_fusion = f32[32,2,18,576]{3,0,2,1:T(8,128)S(1)} fusion(f32[32,4,18,576]{3,0,1,2:T(8,128)} %copy.21, f32[4,576,2,576,1]{3,0,2,1,4:T(4,128)} %bitcast.17, f32[576]{0:T(1024)S(1)} %copy-done.2, f32[32,2,18]{0,2,1:T(8,128)S(1)} %broadcast_subtract_fusion), kind=kOutput, calls=%fused_computation.3 | convolution fusion | flops 18347212800 | bytes 18586368 | tf_op jit(solution)/shard_map/ikac,kcjb->ijab/dot_general | solution.py:8
  381.4 2.3 copy.22
  383.7 75.7 %all_to_all.18 = f32[32,2,18,576]{3,1,2,0:T(2,128)S(1)} all-to-all(f32[32,2,18,576]{3,1,2,0:T(2,128)S(1)} %copy.22), channel_id=1, replica_groups=mesh['row'=32,'col'=16] {'row'}, dimensions={0} | all-to-all | bytes 5308416 | tf_op jit(solution)/shard_map/all_to_all | solution.py:35
  459.3 1.8 copy.23
Async XLA Ops:
  6.5 2.7 copy-start
  6.5 3.6 copy-start.2
  6.5 3.7 copy-start.1
  6.5 241.0 %all-gather.5.cloned.1.call-start = ((), (), s32[]{:S(2)}) async-start(), calls=%async_computation.2 | async-start | bytes 22560768 | tf_op jit(solution)/shard_map/all_gather | solution.py:27
  9.2 341.0 %all-gather.3.cloned.1.call-start = ((), (), s32[]{:S(2)}) async-start(), calls=%async_computation.1 | async-start | bytes 12165120 | tf_op jit(solution)/shard_map/all_gather | solution.py:26
Sparse Core Ops, SparseCore 0:
  9.4 238.0 all-gather.4
  250.6 99.5 all-gather.2
where the time goes:
time: 469 us; the launch traced here: 468 us
  waiting for transfers between devices  322 us (69%)
  blocking collectives  75.7 us (16%)
  matrix products  31.1 us (7%)
  local copies, waits for them, and re-layouts  25.7 us (5%)
  between operations  13.4 us (3%)
    all_gather x1, waiting for transfers between devices, shards(): lax.all_gather(amps, 'col', axis=3, tiled=True)  237 us
    all_gather x1, waiting for transfers between devices, shards(): gathered = lax.all_gather(integrals, 'row', axis=1, tiled=True)  84.8 us
    all_to_all x1, blocking collectives, shards(): lax.all_to_all(scaled, 'row', split_axis=0, concat_axis=2, tiled=True)  75.7 us
    dot_general x1, matrix products, contract(): jnp.einsum('ikac,kcjb->ijab', left, right, precision=lax.Precision.HIGHES...  31.1 us
    all_gather x1, local copies, waits for them, and re-layouts, shards(): lax.all_gather(amps, 'col', axis=3, tiled=True)  18 us
  transfers between devices with their start and end apart: 2, of which 2 were waited for; matrix products, arithmetic and copies ran while one was open for 4% of the time, Pallas kernels for 0%

commit v1 on v0

--- a/solution.py
+++ b/solution.py
@@ -23,7 +23,8 @@
     vir_row = e_vir.shape[0] // row_count
     a_energy = lax.dynamic_slice_in_dim(e_vir, row_index * vir_row, vir_row)
     j_energy = lax.dynamic_slice_in_dim(e_occ, col_index * occ_col, occ_col)
-    gathered = lax.all_gather(integrals, "row", axis=1, tiled=True)
+    repeated = jnp.stack([integrals] * lax.axis_size("row"))
+    gathered = jnp.concatenate(lax.all_to_all(repeated, "row", 0, 0), axis=1)
     contracted = contract(lax.all_gather(amps, "col", axis=3, tiled=True), gathered)
     denom = (
         e_occ[:, None, None, None]

time: 469 us -> 622 us (1.33)
  waiting for transfers between devices: 322 us -> 455 us
  starting transfers between devices: 0.04 us -> 14.7 us
  local copies, waits for them, and re-layouts: 25.7 us -> 36.9 us
    all_to_all x0 -> x1, waiting for transfers between devices: none -> 165 us  [shards(): gathered = jnp.concatenate(lax.all_to_all(repeated, 'row', 0, 0), axis=1)]
    all_gather x1 -> x0, waiting for transfers between devices: 84.8 us -> none  [shards(): gathered = lax.all_gather(integrals, 'row', axis=1, tiled=True)]
    all_gather x1, waiting for transfers between devices: 237 us -> 290 us  [shards(): lax.all_gather(amps, 'col', axis=3, tiled=True)]
    all_to_all x0 -> x1, starting transfers between devices: none -> 14.6 us  [shards(): gathered = jnp.concatenate(lax.all_to_all(repeated, 'row', 0, 0), axis=1)]
    reshape x0 -> x1, local copies, waits for them, and re-layouts: none -> 7.64 us  [shards(): gathered = jnp.concatenate(lax.all_to_all(repeated, 'row', 0, 0), axis=1)]
  transfers between devices with their start and end apart: 2 -> 2, of which waited for: 2 -> 2; matrix products, arithmetic and copies ran while one was open for 4% -> 3% of each run, Pallas kernels for 0% -> 0%
where the time goes in v1:
time: 622 us; the launch traced here: 619 us
  waiting for transfers between devices  455 us (73%)
  blocking collectives  70.9 us (11%)
  local copies, waits for them, and re-layouts  36.9 us (6%)
  matrix products  28.5 us (5%)
  starting transfers between devices  14.7 us (2%)
  between operations  13.5 us (2%)
    all_gather x1, waiting for transfers between devices, shards(): lax.all_gather(amps, 'col', axis=3, tiled=True)  290 us
    all_to_all x1, waiting for transfers between devices, shards(): gathered = jnp.concatenate(lax.all_to_all(repeated, 'row', 0, 0), axis=1)  165 us
    all_to_all x1, blocking collectives, shards(): lax.all_to_all(scaled, 'row', split_axis=0, concat_axis=2, tiled=True)  70.9 us
    dot_general x1, matrix products, contract(): jnp.einsum('ikac,kcjb->ijab', left, right, precision=lax.Precision.HIGHES...  28.5 us
    all_gather x1, local copies, waits for them, and re-layouts, shards(): lax.all_gather(amps, 'col', axis=3, tiled=True)  17.9 us
    all_to_all x1, starting transfers between devices, shards(): gathered = jnp.concatenate(lax.all_to_all(repeated, 'row', 0, 0), axis=1)  14.6 us
  transfers between devices with their start and end apart: 2, of which 2 were waited for; matrix products, arithmetic and copies ran while one was open for 3% of the time, Pallas kernels for 0%

profile of v1, /device:TPU:1, one launch (start us, length us, event | category | flops | bytes accessed | tf_op | source)
XLA Modules:
  0.0 619.2 jit_solution(17316195836790806024)
XLA Ops:
  6.5 5.5 stack.2
  12.0 0.0 copy-start.1
  12.0 0.0 copy-start.3
  12.0 0.0 copy-start.2
  12.0 14.6 %all-to-all-start = ((f32[32,4,18,2,576]{4,3,2,1,0:T(2,128)}), f32[32,4,18,2,576]{4,3,2,1,0:T(2,128)}, u32[]{:S(2)}, u32[]{:S(2)}) async-start(f32[32,4,18,2,576]{4,3,2,1,0:T(2,128)} %stack.2), calls=%async_computation | async-start | bytes 23592960 | tf_op jit(solution)/shard_map/all_to_all | solution.py:27
  26.7 0.0 all-gather.2.cloned.1.call-start
  26.7 0.0 copy-done.1
  26.7 1.6 copy.19
  28.4 0.0 all-gather.2.cloned.1.call-update
  28.4 0.0 copy-done.3
  28.4 0.1 dynamic_slice.7
  28.5 0.0 copy-done.2
  28.5 0.1 dynamic_slice.6
  28.6 0.1 broadcast_add_fusion
  28.6 0.1 broadcast_subtract_fusion
  28.7 289.9 %all-gather.2.cloned.1.call-done = f32[32,4,18,576]{0,1,2,3:T(4,128)} async-done(((f32[32,4,18,36]{0,1,2,3:T(4,128)}), f32[32,4,18,576]{0,1,2,3:T(4,128)}) %all-gather.2.cloned.1.call-update) | async-done | bytes 5308432 | tf_op jit(solution)/shard_map/all_gather | solution.py:28
  318.6 17.9 %copy.21 = f32[32,4,18,576]{3,0,1,2:T(8,128)} copy(f32[32,4,18,576]{0,1,2,3:T(4,128)} %all-gather.2.cloned.1.call-done) | data formatting | bytes 10616832 | tf_op jit(solution)/shard_map/all_gather | solution.py:28
  336.5 164.7 %all-to-all-done = f32[32,4,18,2,576]{4,3,2,1,0:T(2,128)} async-done(((f32[32,4,18,2,576]{4,3,2,1,0:T(2,128)}), f32[32,4,18,2,576]{4,3,2,1,0:T(2,128)}, u32[]{:S(2)}, u32[]{:S(2)}) %all-to-all-start) | async-done | bytes 10616864 | tf_op jit(solution)/shard_map/all_to_all | solution.py:27
  501.2 0.0 copy-start
  501.2 7.6 %copy.18 = f32[4,32,18,2,576]{4,3,2,1,0:T(2,128)S(1)} copy(f32[4,32,18,2,576]{4,3,2,0,1:T(2,128)} %bitcast) | data formatting | bytes 21233664 | tf_op jit(solution)/shard_map/reshape | solution.py:27
  508.8 0.0 copy-done
  508.9 28.5 %bitcast_divide_fusion = f32[32,2,18,576]{3,0,2,1:T(8,128)S(1)} fusion(f32[32,4,18,576]{3,0,1,2:T(8,128)S(1)} %copy-done, f32[4,576,2,576,1]{3,2,1,0,4:T(2,128)S(1)} %bitcast.19, f32[576]{0:T(1024)S(1)} %copy-done.3, f32[32,2,18]{0,2,1:T(8,128)S(1)} %broadcast_subtract_fusion), kind=kOutput, calls=%fused_computation.3 | convolution fusion | flops 18347212800 | bytes 18586368 | tf_op jit(solution)/shard_map/ikac,kcjb->ijab/dot_general | solution.py:8
  537.4 2.3 copy.22
  539.7 70.9 %all_to_all.23 = f32[32,2,18,576]{3,1,2,0:T(2,128)S(1)} all-to-all(f32[32,2,18,576]{3,1,2,0:T(2,128)S(1)} %copy.22), channel_id=1, replica_groups=mesh['row'=32,'col'=16] {'row'}, dimensions={0} | all-to-all | bytes 5308416 | tf_op jit(solution)/shard_map/all_to_all | solution.py:36
  610.6 1.8 copy.23
Async XLA Ops:
  12.0 14.7 %copy-start.1 = (f32[32,4,18,36]{3,1,2,0:T(4,128)S(1)}, f32[32,4,18,36]{3,1,2,0:T(4,128)}, u32[]{:S(2)}) copy-start(f32[32,4,18,36]{3,1,2,0:T(4,128)} %param.4) | copy-start | bytes 995332
  12.0 16.4 %copy-start.3 = (f32[576]{0:T(1024)S(1)}, f32[576]{0:T(1024)}, u32[]{:S(2)}) copy-start(f32[576]{0:T(1024)} %param.7) | copy-start | bytes 6916
  12.0 16.4 %copy-start.2 = (f32[32]{0:T(128)S(1)}, f32[32]{0:T(128)}, u32[]{:S(2)}) copy-start(f32[32]{0:T(128)} %param.6) | copy-start | bytes 388
  12.0 489.1 %all-to-all-start = ((f32[32,4,18,2,576]{4,3,2,1,0:T(2,128)}), f32[32,4,18,2,576]{4,3,2,1,0:T(2,128)}, u32[]{:S(2)}, u32[]{:S(2)}) async-start(f32[32,4,18,2,576]{4,3,2,1,0:T(2,128)} %stack.2), calls=%async_computation | async-start | bytes 23592960 | tf_op jit(solution)/shard_map/all_to_all | solution.py:27
  26.7 291.9 %all-gather.2.cloned.1.call-start = ((), (), s32[]{:S(2)}) async-start(), calls=%async_computation.2 | async-start | bytes 22560768 | tf_op jit(solution)/shard_map/all_gather | solution.py:28
  501.2 7.7 %copy-start = (f32[32,4,18,576]{3,0,1,2:T(8,128)S(1)}, f32[32,4,18,576]{3,0,1,2:T(8,128)}, u32[]{:S(2)}) copy-start(f32[32,4,18,576]{3,0,1,2:T(8,128)} %copy.21) | copy-start | bytes 15925252
Sparse Core Ops, SparseCore 0:
  29.6 288.9 all-gather.1
